TPU v7x, 256 devices: a whole 4x4x8 slice. The times are simulated.
256 devices in a mesh: dp: 8 (over z), tm: 32 (over x, y, core).
Axes of the slice: x: 4, y: 4, z: 8, core: 2. Of those that a mesh axis runs over, the one named last changes fastest.
Arguments:
- clips: bfloat16 [8, 128, 16, 16, 128], P('dp', 'tm'), may hold values from -6 to 6
- segment_ids: int32 [8, 128], P('dp'), may hold values from 0 to 3, never falling along the last dimension, each value on 1 to 64 neighbouring positions
- conv_weight: bfloat16 [3456, 128], replicated, may hold values from -0.109375 to 0.109375
- cotangent: bfloat16 [8, 128, 16, 16, 128], P('dp', 'tm'), may hold values from -6 to 6
Outputs:
- activated: bfloat16 [8, 128, 16, 16, 128], P('dp', 'tm')
- grad_clips: bfloat16 [8, 128, 16, 16, 128], P('dp', 'tm')
- grad_weight: float32 [3456, 128], P('tm')
Inputs may be any that keep to these rules, and one draw needn't show every extreme that they name: segment_ids never fall along a sequence; each clip has 1 to 64 frames and one has exactly that many.
All inputs are finite; a program needn't handle non-finite values.
Results may differ from a plain program's by a relative error of at most 0.013.
Values may be sent and summed in bfloat16 or wider, within the bound.
No kernel may reach another device: no remote copies, remote signals or barrier semaphores. Data moves between devices by JAX's collectives and lax.ppermute only.
A program may use at most 64 MiB of HBM per device.

v0:
```python
import jax
import jax.numpy as jnp
from jax import lax
from jax.sharding import PartitionSpec as P


def from_behind(value, axis, steps):
    count = lax.axis_size(axis)
    leading, last = (max(0, -steps), min(count, count - steps))
    return lax.ppermute(value, axis, [(source, source + steps) for source in range(leading, last)])


def per_device(clips, segment_ids, conv_weight, cotangent):
    nfr = clips.shape[1]
    hh = clips.shape[2]
    ww = clips.shape[3]
    cc = clips.shape[4]
    rows = nfr * hh * ww
    earlier = from_behind(clips[:, nfr - 2 :], "tm", 1)
    extended = jnp.concatenate([earlier, clips], axis=1)[0]
    segrow = segment_ids[0]
    segp = jnp.concatenate([jnp.full((2,), -1, jnp.int32), segrow, jnp.full((2,), -2, jnp.int32)])
    start = lax.axis_index("tm") * nfr
    seglocal = lax.dynamic_slice_in_dim(segp, start, nfr + 4, 0)
    own = seglocal[2 : 2 + nfr]
    patches = []
    pre = jnp.zeros((rows, cc), jnp.float32)
    for kt in range(3):
        moved = extended[kt : kt + nfr]
        keep = seglocal[kt : kt + nfr] == own
        moved = jnp.where(keep[:, None, None, None], moved, jnp.zeros_like(moved))
        padded = jnp.pad(moved, ((0, 0), (1, 1), (1, 1), (0, 0)))
        pieces = [padded[:, ky : ky + hh, kx : kx + ww] for ky in range(3) for kx in range(3)]
        patch = jnp.concatenate(pieces, axis=3).reshape(rows, 9 * cc)
        patches.append(patch)
        pre = pre + jnp.dot(
            patch, conv_weight[kt * 9 * cc : (kt + 1) * 9 * cc], preferred_element_type=jnp.float32
        )
    activated = jax.nn.silu(pre).astype(jnp.bfloat16).reshape(clips.shape)
    sig = jax.nn.sigmoid(pre)
    grad_pre = (
        cotangent.reshape(rows, cc).astype(jnp.float32) * sig * (1.0 + pre * (1.0 - sig))
    ).astype(jnp.bfloat16)
    count = lax.axis_size("dp") * lax.axis_size("tm") * rows
    grad_local = jnp.concatenate(
        [
            lax.dot_general(
                patch, grad_pre, (((0,), (0,)), ((), ())), preferred_element_type=jnp.float32
            )
            for patch in patches
        ],
        axis=0,
    )
    grad_local = grad_local / jnp.sqrt(jnp.float32(count))
    frames_grad = grad_pre.reshape(1, nfr, hh, ww, cc)
    later_part = from_behind(frames_grad[:, :2], "tm", -1)
    grad_ext = jnp.concatenate([frames_grad, later_part], axis=1)[0]
    summed = jnp.zeros((rows, 9 * cc), jnp.float32)
    for kt in range(3):
        d = 2 - kt
        later = grad_ext[d : d + nfr]
        keep = seglocal[2 + d : 2 + d + nfr] == own
        later = jnp.where(keep[:, None, None, None], later, jnp.zeros_like(later)).reshape(rows, cc)
        summed = summed + lax.dot_general(
            later,
            conv_weight[kt * 9 * cc : (kt + 1) * 9 * cc],
            (((1,), (1,)), ((), ())),
            preferred_element_type=jnp.float32,
        )
    summed = summed.reshape(nfr, hh, ww, 9, cc)
    canvas = jnp.zeros((nfr, hh + 2, ww + 2, cc), jnp.float32)
    for ky in range(3):
        for kx in range(3):
            canvas = canvas.at[:, ky : ky + hh, kx : kx + ww].add(summed[:, :, :, ky * 3 + kx])
    grad_clips = canvas[:, 1:-1, 1:-1].astype(jnp.bfloat16).reshape(clips.shape)
    share_rows = grad_local.shape[0] // lax.axis_size("tm")
    total = lax.psum(grad_local, ("dp", "tm"))
    grad_weight = lax.dynamic_slice_in_dim(total, lax.axis_index("tm") * share_rows, share_rows, 0)
    return (activated, grad_clips, grad_weight)


def solution(mesh):
    return jax.shard_map(
        per_device,
        mesh=mesh,
        in_specs=(
            P("dp", "tm", None, None, None),
            P("dp", None),
            P(),
            P("dp", "tm", None, None, None),
        ),
        out_specs=(P("dp", "tm", None, None, None), P("dp", "tm", None, None, None), P("tm", None)),
        check_vma=False,
    )
```

profile of v0, /device:TPU:2, one launch (start us, length us, event | category | flops | bytes accessed | tf_op | source)
XLA Modules:
  0.0 301.6 jit_solution(8584760968547292022)
XLA Ops:
  7.2 0.9 slice.482
  8.2 1.9 collective-permute-start
  11.0 2.5 pad_slice_fusion
  20.5 1.6 fusion.3
  22.9 0.8 fusion.36
  23.7 0.8 fusion.35
  24.6 5.8 %collective-permute-start.1 = (bf16[1,2,16,16,128]{4,3,2,1,0:T(8,128)(2,1)S(1)}, bf16[1,2,16,16,128]{4,3,2,1,0:T(8,128)(2,1)S(1)}, u32[]{:S(2)}, u32[]{:S(2)}) collective-permute-start(bf16[1,2,16,16,128]{4,3,2,1,0:T(8,128)(2,1)S(1)} %slice.545), channel_id=1, source_target_pairs={{1,0},{2,1},{3,2},{4,3},{5,4},{6,5},{7,6},{8,7},{9,8},{10,9},{11,1... | collective-permute-start | bytes 393224 | tf_op jit(solution)/shard_map/ppermute | solution.py:10
  30.4 1.3 maximum_multiply_fusion
  31.7 1.0 collective-permute-done.1
  34.7 3.0 convolution_add_fusion
  37.7 6.9 %reshape.439 = f32[4,16,16,9,128]{4,3,2,1,0:T(8,128)} reshape(f32[1024,1152]{1,0:T(8,128)} %convolution_add_fusion) | data formatting | bytes 9437184 | tf_op jit(solution)/shard_map/reshape | solution.py:70
  44.6 16.6 %fusion.32 = (f32[4,16,16,1,128]{4,3,2,1,0:T(1,128)S(1)}, f32[4,16,16,1,128]{4,3,2,1,0:T(1,128)S(1)}, f32[4,16,16,1,128]{4,3,2,1,0:T(1,128)S(1)}, f32[4,16,16,1,...) fusion(f32[4,16,16,9,128]{4,3,2,1,0:T(8,128)} %reshape.439), kind=kLoop, calls=%fused_computation.101 | loop fusion | bytes 9437184 | tf_op jit(solution)/shard_map/slice | solution.py:74
  61.2 2.2 dynamic-slice_add_fusion
  63.4 4.3 %scatter-add.31 = f32[4,18,18,128]{3,2,1,0:T(8,128)S(1)} dynamic-update-slice(f32[4,18,18,128]{3,2,1,0:T(8,128)S(1)} %scatter-add.30, f32[4,16,16,128]{3,2,1,0:T(8,128)} %dynamic-slice_add_fusion, s32[]{:T(128)} %constant.283.clone.1, s32[]{:T(128)} %bitcast.21, s32[]{:T(128)} %bitcast.22, s32[]{:T(128)} %constant.283.clone.1) | dynamic-update-slice | bytes 1048580 | tf_op jit(solution)/shard_map/scatter-add | solution.py:74
  67.7 3.8 %add_select_fusion = f32[4,16,16,128]{3,2,1,0:T(8,128)} fusion(f32[4,16,16,128]{3,2,1,0:T(8,128)} %bitcast.89, f32[4,18,18,128]{3,2,1,0:T(8,128)S(1)} %scatter-add.31, s32[]{:T(128)} %bitcast.24, s32[]{:T(128)} %bitcast.25, pred[]{:T(512)} %and_reduce_fusion), kind=kLoop, calls=%fused_computation.5 | loop fusion | flops 262144 | bytes 1572873 | tf_op jit(solution)/shard_map/select.11
  71.5 4.3 %scatter-add.34 = f32[4,18,18,128]{3,2,1,0:T(8,128)S(1)} dynamic-update-slice(f32[4,18,18,128]{3,2,1,0:T(8,128)S(1)} %scatter-add.31, f32[4,16,16,128]{3,2,1,0:T(8,128)} %add_select_fusion, s32[]{:T(128)} %constant.283.clone.1, s32[]{:T(128)} %bitcast.24, s32[]{:T(128)} %bitcast.25, s32[]{:T(128)} %constant.283.clone.1) | dynamic-update-slice | bytes 1048580 | tf_op jit(solution)/shard_map/scatter-add | solution.py:74
  75.8 1.1 fusion.1
  77.0 0.9 slice_add_fusion.4
  77.9 3.0 %scatter-add.36 = f32[4,18,18,128]{3,2,1,0:T(8,128)S(1)} dynamic-update-slice(f32[4,18,18,128]{3,2,1,0:T(8,128)S(1)} %fusion.1, f32[4,16,16,128]{3,2,1,0:T(8,128)} %slice_add_fusion.4, s32[]{:T(128)} %constant.283.clone.1, s32[]{:T(128)} %constant.292.clone.1, s32[]{:T(128)} %constant.292.clone.1, s32[]{:T(128)} %constant.283.clone.1) | dynamic-update-slice | bytes 1048580 | tf_op jit(solution)/shard_map/scatter-add | solution.py:74
  81.0 1.7 scatter-add.39
  82.8 1.7 scatter-add.41
  84.6 1.7 scatter-add.44
  87.0 206.2 %all-reduce.6.cloned.1.call-done = f32[3456,128]{1,0:T(8,128)} async-done(((f32[3456,128]{1,0:T(8,128)}), f32[3456,128]{1,0:T(8,128)}) %all-reduce.6.cloned.1.call-update) | async-done | bytes 1769488 | tf_op jit(solution)/shard_map/psum | solution.py:77
  293.3 1.5 constant_dynamic-slice_fusion
  (69 shorter events, 11.6 us)
Async XLA Ops:
  7.2 7.2 %copy-start = (bf16[1,4,16,16,128]{4,3,2,1,0:T(8,128)(2,1)S(1)}, bf16[1,4,16,16,128]{4,3,2,1,0:T(8,128)(2,1)}, u32[]{:S(2)}) copy-start(bf16[1,4,16,16,128]{4,3,2,1,0:T(8,128)(2,1)} %param.22) | copy-start | bytes 786436
  7.2 286.1 %all-reduce.6.cloned.1.call-start = ((), (), s32[]{:S(2)}) async-start(), calls=%async_computation | async-start | bytes 3538944 | tf_op jit(solution)/shard_map/psum | solution.py:77
  8.2 8.4 %collective-permute-start = (bf16[1,2,16,16,128]{4,3,2,1,0:T(8,128)(2,1)S(1)}, bf16[1,2,16,16,128]{4,3,2,1,0:T(8,128)(2,1)S(1)}, u32[]{:S(2)}, u32[]{:S(2)}) collective-permute-start(bf16[1,2,16,16,128]{4,3,2,1,0:T(8,128)(2,1)S(1)} %slice.482), channel_id=1, source_target_pairs={{0,1},{1,2},{2,3},{3,4},{4,5},{5,6},{6,7},{7,8},{8,9},{9,10},{10,1... | collective-permute-start | bytes 393224 | tf_op jit(solution)/shard_map/ppermute | solution.py:10
  13.5 1.2 copy-start.2
  17.6 1.2 copy-start.1
  19.5 1.0 copy-start.3
  24.6 8.1 %collective-permute-start.1 = (bf16[1,2,16,16,128]{4,3,2,1,0:T(8,128)(2,1)S(1)}, bf16[1,2,16,16,128]{4,3,2,1,0:T(8,128)(2,1)S(1)}, u32[]{:S(2)}, u32[]{:S(2)}) collective-permute-start(bf16[1,2,16,16,128]{4,3,2,1,0:T(8,128)(2,1)S(1)} %slice.545), channel_id=1, source_target_pairs={{1,0},{2,1},{3,2},{4,3},{5,4},{6,5},{7,6},{8,7},{9,8},{10,9},{11,1... | collective-permute-start | bytes 393224 | tf_op jit(solution)/shard_map/ppermute | solution.py:10
Sparse Core Ops, SparseCore 0:
  31.9 261.3 all-reduce.5
where the time goes:
time: 302 us
  waiting for transfers between devices  207 us (69%)
  local copies, waits for them, and re-layouts  50.1 us (17%)
  between operations  14.5 us (5%)
  other arithmetic  11.7 us (4%)
  matrix products  10.2 us (3%)
  starting transfers between devices  7.76 us (3%)
    psum x1, waiting for transfers between devices, per_device(): total = lax.psum(grad_local, ('dp', 'tm'))  206 us
    scatter-add x7, local copies, waits for them, and re-layouts, per_device(): canvas.at[:, ky:ky + hh, kx:kx + ww].add(summed[:, :, :, ky * 3 + kx])  16.8 us
    slice x1, local copies, waits for them, and re-layouts, per_device(): summed[:, :, :, ky * 3 + kx]  16.6 us
    ppermute x2, starting transfers between devices, from_behind(): lax.ppermute(value, axis, [(source, source + steps) for source in range(l...  7.72 us
    reshape x1, local copies, waits for them, and re-layouts, per_device(): summed = summed.reshape(nfr, hh, ww, 9, cc)  6.85 us
  transfers between devices with their start and end apart: 3, of which 3 were waited for; matrix products, arithmetic and copies ran while one was open for 20% of the time, Pallas kernels for 0%

commit v1 on v0

--- a/solution.py
+++ b/solution.py
@@ -74,7 +74,7 @@
             canvas = canvas.at[:, ky : ky + hh, kx : kx + ww].add(summed[:, :, :, ky * 3 + kx])
     grad_clips = canvas[:, 1:-1, 1:-1].astype(jnp.bfloat16).reshape(clips.shape)
     share_rows = grad_local.shape[0] // lax.axis_size("tm")
-    total = lax.psum(grad_local, ("dp", "tm"))
+    total = lax.psum(lax.psum(grad_local, "dp"), "tm")
     grad_weight = lax.dynamic_slice_in_dim(total, lax.axis_index("tm") * share_rows, share_rows, 0)
     return (activated, grad_clips, grad_weight)
 

time: 302 us -> 241 us (0.80)
  waiting for transfers between devices: 207 us -> 145 us
    psum x1 -> x2, waiting for transfers between devices: 206 us -> 144 us  [per_device(): total = lax.psum(lax.psum(grad_local, 'dp'), 'tm')]
  transfers between devices with their start and end apart: 3 -> 4, of which waited for: 3 -> 4; matrix products, arithmetic and copies ran while one was open for 20% -> 26% of each run, Pallas kernels for 0% -> 0%
where the time goes in v1:
time: 241 us; the launch traced here: 239 us
  waiting for transfers between devices  145 us (60%)
  local copies, waits for them, and re-layouts  50.1 us (21%)
  between operations  14.5 us (6%)
  other arithmetic  11.7 us (5%)
  matrix products  10.2 us (4%)
  starting transfers between devices  7.8 us (3%)
    psum x2, waiting for transfers between devices, per_device(): total = lax.psum(lax.psum(grad_local, 'dp'), 'tm')  144 us
    scatter-add x7, local copies, waits for them, and re-layouts, per_device(): canvas.at[:, ky:ky + hh, kx:kx + ww].add(summed[:, :, :, ky * 3 + kx])  16.8 us
    slice x1, local copies, waits for them, and re-layouts, per_device(): summed[:, :, :, ky * 3 + kx]  16.6 us
    ppermute x2, starting transfers between devices, from_behind(): lax.ppermute(value, axis, [(source, source + steps) for source in range(l...  7.54 us
    reshape x1, local copies, waits for them, and re-layouts, per_device(): summed = summed.reshape(nfr, hh, ww, 9, cc)  6.86 us
  transfers between devices with their start and end apart: 4, of which 4 were waited for; matrix products, arithmetic and copies ran while one was open for 26% of the time, Pallas kernels for 0%

profile of v1, /device:TPU:2, one launch (start us, length us, event | category | flops | bytes accessed | tf_op | source)
XLA Modules:
  0.0 239.0 jit_solution(15635994529771364323)
XLA Ops:
  7.2 0.9 slice.482
  8.2 1.9 collective-permute-start
  11.0 2.5 %pad_slice_fusion = (bf16[4,16,16,128]{3,2,1,0:T(8,128)(2,1)S(1)}, bf16[4,16,16,128]{3,2,1,0:T(8,128)(2,1)S(1)}, bf16[4,16,16,128]{3,2,1,0:T(8,128)(2,1)S(1)}, b...) fusion(bf16[4,16,16,128]{3,2,1,0:T(8,128)(2,1)} %bitcast.81), kind=kLoop, calls=%fused_computation.6 | loop fusion | bytes 2359296 | tf_op jit(solution)/shard_map/slice | solution.py:33
  20.5 1.6 fusion.3
  23.7 0.8 fusion.35
  24.6 5.6 %collective-permute-start.1 = (bf16[1,2,16,16,128]{4,3,2,1,0:T(8,128)(2,1)S(1)}, bf16[1,2,16,16,128]{4,3,2,1,0:T(8,128)(2,1)S(1)}, u32[]{:S(2)}, u32[]{:S(2)}) collective-permute-start(bf16[1,2,16,16,128]{4,3,2,1,0:T(8,128)(2,1)S(1)} %slice.545), channel_id=1, source_target_pairs={{1,0},{2,1},{3,2},{4,3},{5,4},{6,5},{7,6},{8,7},{9,8},{10,9},{11,1... | collective-permute-start | bytes 393224 | tf_op jit(solution)/shard_map/ppermute | solution.py:10
  30.2 1.3 maximum_multiply_fusion
  31.8 0.9 collective-permute-done.1
  34.7 3.0 %convolution_add_fusion = f32[1024,1152]{1,0:T(8,128)} fusion(f32[1024,1152]{1,0:T(8,128)S(1)} %convolution_add_fusion.1, bf16[1024,128]{1,0:T(8,128)(2,1)S(1)} %get-tuple-element.120, bf16[3456,128]{1,0:T(8,128)(2,1)S(1)} %copy-done.1), kind=kOutput, calls=%fused_computation | convolution fusion | flops 303169536 | bytes 9994240 | tf_op jit(solution)/shard_map/dot_general | solution.py:64
  37.7 6.9 %reshape.439 = f32[4,16,16,9,128]{4,3,2,1,0:T(8,128)} reshape(f32[1024,1152]{1,0:T(8,128)} %convolution_add_fusion) | data formatting | bytes 9437184 | tf_op jit(solution)/shard_map/reshape | solution.py:70
  44.6 16.6 %fusion.32 = (f32[4,16,16,1,128]{4,3,2,1,0:T(1,128)S(1)}, f32[4,16,16,1,128]{4,3,2,1,0:T(1,128)S(1)}, f32[4,16,16,1,128]{4,3,2,1,0:T(1,128)S(1)}, f32[4,16,16,1,...) fusion(f32[4,16,16,9,128]{4,3,2,1,0:T(8,128)} %reshape.439), kind=kLoop, calls=%fused_computation.101 | loop fusion | bytes 9437184 | tf_op jit(solution)/shard_map/slice | solution.py:74
  61.2 2.2 dynamic-slice_add_fusion
  63.4 4.3 %scatter-add.31 = f32[4,18,18,128]{3,2,1,0:T(8,128)S(1)} dynamic-update-slice(f32[4,18,18,128]{3,2,1,0:T(8,128)S(1)} %scatter-add.30, f32[4,16,16,128]{3,2,1,0:T(8,128)} %dynamic-slice_add_fusion, s32[]{:T(128)} %constant.283.clone.1, s32[]{:T(128)} %bitcast.21, s32[]{:T(128)} %bitcast.22, s32[]{:T(128)} %constant.283.clone.1) | dynamic-update-slice | bytes 1048580 | tf_op jit(solution)/shard_map/scatter-add | solution.py:74
  67.7 3.8 %add_select_fusion = f32[4,16,16,128]{3,2,1,0:T(8,128)} fusion(f32[4,16,16,128]{3,2,1,0:T(8,128)} %bitcast.89, f32[4,18,18,128]{3,2,1,0:T(8,128)S(1)} %scatter-add.31, s32[]{:T(128)} %bitcast.24, s32[]{:T(128)} %bitcast.25, pred[]{:T(512)} %and_reduce_fusion), kind=kLoop, calls=%fused_computation.5 | loop fusion | flops 262144 | bytes 1572873 | tf_op jit(solution)/shard_map/select.11
  71.5 4.3 %scatter-add.34 = f32[4,18,18,128]{3,2,1,0:T(8,128)S(1)} dynamic-update-slice(f32[4,18,18,128]{3,2,1,0:T(8,128)S(1)} %scatter-add.31, f32[4,16,16,128]{3,2,1,0:T(8,128)} %add_select_fusion, s32[]{:T(128)} %constant.283.clone.1, s32[]{:T(128)} %bitcast.24, s32[]{:T(128)} %bitcast.25, s32[]{:T(128)} %constant.283.clone.1) | dynamic-update-slice | bytes 1048580 | tf_op jit(solution)/shard_map/scatter-add | solution.py:74
  75.8 1.1 fusion.1
  77.0 0.9 slice_add_fusion.4
  77.9 3.0 %scatter-add.36 = f32[4,18,18,128]{3,2,1,0:T(8,128)S(1)} dynamic-update-slice(f32[4,18,18,128]{3,2,1,0:T(8,128)S(1)} %fusion.1, f32[4,16,16,128]{3,2,1,0:T(8,128)} %slice_add_fusion.4, s32[]{:T(128)} %constant.283.clone.1, s32[]{:T(128)} %constant.292.clone.1, s32[]{:T(128)} %constant.292.clone.1, s32[]{:T(128)} %constant.283.clone.1) | dynamic-update-slice | bytes 1048580 | tf_op jit(solution)/shard_map/scatter-add | solution.py:74
  81.0 1.7 scatter-add.39
  82.6 29.8 %all-reduce.7.cloned.1.call-done = f32[3456,128]{1,0:T(8,128)} async-done(((f32[3456,128]{1,0:T(8,128)}), f32[3456,128]{1,0:T(8,128)}) %all-reduce.7.cloned.1.call-update) | async-done | bytes 1769488 | tf_op jit(solution)/shard_map/psum | solution.py:77
  112.7 1.7 scatter-add.41
  114.4 1.7 scatter-add.44
  116.9 113.9 %all-reduce.9.cloned.1.call-done = f32[3456,128]{1,0:T(8,128)} async-done(((f32[3456,128]{1,0:T(8,128)}), f32[3456,128]{1,0:T(8,128)}) %all-reduce.9.cloned.1.call-update) | async-done | bytes 1769488 | tf_op jit(solution)/shard_map/psum | solution.py:77
  230.7 1.5 constant_dynamic-slice_fusion
  (72 shorter events, 12.7 us)
Async XLA Ops:
  7.2 7.2 %copy-start = (bf16[1,4,16,16,128]{4,3,2,1,0:T(8,128)(2,1)S(1)}, bf16[1,4,16,16,128]{4,3,2,1,0:T(8,128)(2,1)}, u32[]{:S(2)}) copy-start(bf16[1,4,16,16,128]{4,3,2,1,0:T(8,128)(2,1)} %param.22) | copy-start | bytes 786436
  7.2 105.3 %all-reduce.7.cloned.1.call-start = ((), (), s32[]{:S(2)}) async-start(), calls=%async_computation | async-start | bytes 3538944 | tf_op jit(solution)/shard_map/psum | solution.py:77
  8.2 8.4 %collective-permute-start = (bf16[1,2,16,16,128]{4,3,2,1,0:T(8,128)(2,1)S(1)}, bf16[1,2,16,16,128]{4,3,2,1,0:T(8,128)(2,1)S(1)}, u32[]{:S(2)}, u32[]{:S(2)}) collective-permute-start(bf16[1,2,16,16,128]{4,3,2,1,0:T(8,128)(2,1)S(1)} %slice.482), channel_id=1, source_target_pairs={{0,1},{1,2},{2,3},{3,4},{4,5},{5,6},{6,7},{7,8},{8,9},{9,10},{10,1... | collective-permute-start | bytes 393224 | tf_op jit(solution)/shard_map/ppermute | solution.py:10
  13.5 1.2 copy-start.2
  17.6 1.2 copy-start.1
  19.5 1.0 copy-start.3
  24.6 8.1 %collective-permute-start.1 = (bf16[1,2,16,16,128]{4,3,2,1,0:T(8,128)(2,1)S(1)}, bf16[1,2,16,16,128]{4,3,2,1,0:T(8,128)(2,1)S(1)}, u32[]{:S(2)}, u32[]{:S(2)}) collective-permute-start(bf16[1,2,16,16,128]{4,3,2,1,0:T(8,128)(2,1)S(1)} %slice.545), channel_id=1, source_target_pairs={{1,0},{2,1},{3,2},{4,3},{5,4},{6,5},{7,6},{8,7},{9,8},{10,9},{11,1... | collective-permute-start | bytes 393224 | tf_op jit(solution)/shard_map/ppermute | solution.py:10
  31.6 199.2 %all-reduce.9.cloned.1.call-start = ((), (), s32[]{:S(2)}) async-start(), calls=%async_computation.1 | async-start | bytes 3538944 | tf_op jit(solution)/shard_map/psum | solution.py:77
Sparse Core Ops, SparseCore 0:
  31.7 80.7 all-reduce.6
  115.8 114.8 all-reduce.8
